TPU v7x, 256 devices: a whole 4x4x8 slice. The times are simulated.
256 devices in a mesh: grp: 32 (over z, x), tp: 8 (over y, core).
Axes of the slice: x: 4, y: 4, z: 8, core: 2. Of those that a mesh axis runs over, the one named last changes fastest.
Arguments:
- tokens: bfloat16 [32768, 2048], P('grp'), may hold values from -6 to 6
- norm_gain: float32 [2048], replicated, may hold values from 0.5 to 7
- w_qkv: bfloat16 [2048, 3, 2048], P(None, None, 'tp'), may hold values from -0.125 to 0.125
- w_out: bfloat16 [2048, 2048], P('tp'), may hold values from -0.125 to 0.125
- a_in: bfloat16 [64, 2048, 48], P('grp', 'tp'), may hold values from -0.125 to 0.125
- b_in: bfloat16 [64, 3, 16, 2048], P('grp', None, None, 'tp'), may hold values from -1.5 to 1.5
- a_out: bfloat16 [64, 2048, 16], P('grp', 'tp'), may hold values from -0.125 to 0.125
- b_out: bfloat16 [64, 16, 2048], P('grp', None, 'tp'), may hold values from -1.5 to 1.5
- req_len: int32 [32, 4], replicated, may hold values from 1 to 512, 1024 in all within a row
- req_adapter: int32 [32, 4], replicated, may hold values from 0 to 63, as said below
- holder: int32 [64], replicated, may hold values from 0 to 63, each once
- page_table: int32 [32, 8], P('grp'), may hold values from 0 to 7, each once within a row
Outputs:
- layer_out: bfloat16 [32768, 2048], P('grp', 'tp')
- kv_pages: bfloat16 [256, 2, 128, 2048], P('grp', None, None, 'tp')
Inputs may be any that keep to these rules, and one draw needn't show every extreme that they name: `req_adapter`: exactly 16 different adapters appear among all requests.
All inputs are finite; a program needn't handle non-finite values.
Results may differ from a plain program's by a relative error of at most 0.017.
The roundings to bfloat16 on the way count: a program that leaves them out, or rounds other values in their place, can miss the bound.
Values may be sent and summed in bfloat16 or wider, within the bound.
No kernel may reach another device: no remote copies, remote signals or barrier semaphores. Data moves between devices by JAX's collectives and lax.ppermute only.
A program may use at most 128 MiB of HBM per device.

v0:
```python
import math
import jax
import jax.numpy as jnp
from jax import lax
from jax.sharding import PartitionSpec as P

HD = 128
PAGE = 128
EPSILON = 1e-05
THETA = 10000.0


def shifted(block, axis, distance):
    devices = range(lax.axis_size(axis))
    route = [(i - distance, i) for i in devices if i - distance in devices]
    return lax.ppermute(block, axis, route)


USED = 16


def xor_allreduce(value, axis):
    count = lax.axis_size(axis)
    step = 1
    while step < count:
        route = [(i, i ^ step) for i in range(count)]
        value = value + lax.ppermute(value, axis, route)
        step *= 2
    return value


def fetch_adapters(stores, req_adapter, holder, wanted, group_id):
    held = stores[0].shape[0]
    total = holder.shape[0]
    names = jnp.arange(total, dtype=jnp.int32)
    used = jnp.any(req_adapter.reshape(-1)[:, None] == names[None, :], axis=0)
    rank = jnp.cumsum(used.astype(jnp.int32)) - 1
    picks = jnp.arange(USED, dtype=jnp.int32)
    hit = used[None, :] & (rank[None, :] == picks[:, None])
    chosen = jnp.sum(jnp.where(hit, names[None, :], 0), axis=1)
    slots = holder[chosen]
    mine = slots // held == group_id
    local_idx = slots % held
    flat = jnp.concatenate([s.reshape(held, -1) for s in stores], axis=1)
    compact = jnp.where(mine[:, None], jnp.take(flat, local_idx, axis=0), jnp.zeros((), flat.dtype))
    compact = lax.psum(compact, "grp")
    mine_rows = jnp.take(compact, rank[wanted], axis=0)
    out = []
    at = 0
    for s in stores:
        size = math.prod(s.shape[1:])
        out.append(mine_rows[:, at : at + size].reshape((wanted.shape[0],) + s.shape[1:]))
        at += size
    return tuple(out)


def rms_norm(token_rows, norm_gain):
    values = token_rows.astype(jnp.float32)
    norm_scale = lax.rsqrt(jnp.mean(values * values, axis=-1, keepdims=True) + EPSILON)
    return (values * norm_scale * norm_gain).astype(jnp.bfloat16)


def request_layout(lengths, offset, tok_count):
    end_at = jnp.cumsum(lengths)
    starts = end_at - lengths
    row_ids = jnp.arange(tok_count, dtype=jnp.int32)
    segment = jnp.sum((row_ids[:, None] >= end_at[None, :]).astype(jnp.int32), axis=1)
    member = segment[:, None] == jnp.arange(lengths.shape[0], dtype=jnp.int32)[None, :]
    begin_at = jnp.sum(jnp.where(member, starts[None, :], 0), axis=1)
    position = row_ids - begin_at + jnp.where(segment == 0, offset, 0)
    return (segment, member, position)


def rotate(head_rows, position, head_dim):
    half_dim = head_dim // 2
    frequency = THETA ** (-(jnp.arange(half_dim, dtype=jnp.float32) * (2.0 / head_dim)))
    angles = position.astype(jnp.float32)[:, None] * frequency[None, :]
    cosine = jnp.cos(angles)[:, None, :]
    sine_part = jnp.sin(angles)[:, None, :]
    lower_half = head_rows[..., :half_dim]
    upper_half = head_rows[..., half_dim:]
    return jnp.concatenate(
        [
            lower_half * cosine - upper_half * sine_part,
            upper_half * cosine + lower_half * sine_part,
        ],
        axis=-1,
    )


def local(
    tokens,
    norm_gain,
    w_qkv,
    w_out,
    a_in,
    b_in,
    a_out,
    b_out,
    req_len,
    req_adapter,
    holder,
    page_table,
):
    tok_count = tokens.shape[0]
    local_width = w_out.shape[0]
    local_heads = local_width // HD
    req_count = req_len.shape[1]
    rank_dim = a_out.shape[2]
    group_id = lax.axis_index("grp")
    tp_id = lax.axis_index("tp")
    lengths = lax.dynamic_index_in_dim(req_len, group_id, 0, keepdims=False)
    earlier = lax.dynamic_index_in_dim(req_len, jnp.maximum(group_id - 1, 0), 0, keepdims=False)
    continued = group_id > 0
    prev_len = earlier[req_count - 1]
    offset = jnp.where(continued, prev_len, 0)
    segment, member, position = request_layout(lengths, offset, tok_count)
    wanted = lax.dynamic_index_in_dim(req_adapter, group_id, 0, keepdims=False)
    sel_in, sel_up, sel_odown, sel_oup = fetch_adapters(
        (a_in, b_in, a_out, b_out), req_adapter, holder, wanted, group_id
    )
    member_f = member.astype(jnp.float32)
    pick_bf = member.astype(jnp.bfloat16)
    normed = rms_norm(tokens, norm_gain)
    own_cols = lax.dynamic_slice_in_dim(normed, tp_id * local_width, local_width, 1)
    down_f = jnp.einsum("td,rdk->trk", own_cols, sel_in, preferred_element_type=jnp.float32)
    lowrank_f = xor_allreduce(jnp.sum(down_f * member_f[:, :, None], axis=1), "tp")
    lowrank = lowrank_f.astype(jnp.bfloat16)
    spread = (pick_bf[:, :, None] * lowrank[:, None, :]).reshape(tok_count, req_count, 3, rank_dim)
    delta_qkv = jnp.einsum("trck,rckd->tcd", spread, sel_up, preferred_element_type=jnp.float32)
    base_qkv = jnp.dot(
        normed, w_qkv.reshape(w_qkv.shape[0], 3 * local_width), preferred_element_type=jnp.float32
    )
    qkv = (base_qkv.reshape(tok_count, 3, local_width) + delta_qkv).reshape(
        tok_count, 3, local_heads, HD
    )
    query_rows = rotate(qkv[:, 0], position, HD).astype(jnp.bfloat16)
    key_rows = rotate(qkv[:, 1], position, HD).astype(jnp.bfloat16).reshape(tok_count, local_width)
    value_rows = qkv[:, 2].astype(jnp.bfloat16).reshape(tok_count, local_width)
    row_ids = jnp.arange(tok_count, dtype=jnp.int32)
    far_key, far_value = shifted((key_rows, value_rows), "grp", 1)
    far_ok = continued & (segment[:, None] == 0) & (row_ids[None, :] >= tok_count - prev_len)
    far_count = far_key.shape[0]
    near_ok = (segment[:, None] == segment[None, :]) & (row_ids[None, :] <= row_ids[:, None])
    allowed = jnp.concatenate([far_ok, near_ok], axis=1)
    key_all = jnp.concatenate([far_key, key_rows], axis=0).reshape(
        far_count + tok_count, local_heads, HD
    )
    value_all = jnp.concatenate([far_value, value_rows], axis=0).reshape(
        far_count + tok_count, local_heads, HD
    )
    score_scale = 1.0 / math.sqrt(HD)
    scores = (
        jnp.einsum("thd,shd->hts", query_rows, key_all, preferred_element_type=jnp.float32)
        * score_scale
    )
    scores = jnp.where(allowed[None], scores, -jnp.inf)
    row_top = jnp.max(scores, axis=-1, keepdims=True)
    weights = jnp.exp(scores - row_top)
    weights_bf = (weights / jnp.sum(weights, axis=-1, keepdims=True)).astype(jnp.bfloat16)
    mixed_heads = jnp.einsum(
        "hts,shd->thd", weights_bf, value_all, preferred_element_type=jnp.float32
    )
    attended = mixed_heads.astype(jnp.bfloat16).reshape(tok_count, local_width)
    partial_value = jnp.dot(attended, w_out, preferred_element_type=jnp.float32)
    down_o = jnp.einsum("td,rdk->trk", attended, sel_odown, preferred_element_type=jnp.float32)
    low_part = jnp.sum(down_o * member_f[:, :, None], axis=1).astype(jnp.bfloat16)
    n_tp = lax.axis_size("tp")
    packed = jnp.concatenate(
        [
            partial_value.astype(jnp.bfloat16).reshape(tok_count, n_tp, local_width),
            jnp.broadcast_to(low_part[:, None, :], (tok_count, n_tp, rank_dim)),
        ],
        axis=2,
    ).reshape(tok_count, n_tp * (local_width + rank_dim))
    summed = lax.psum_scatter(packed, "tp", scatter_dimension=1, tiled=True)
    base_out = summed[:, :local_width].astype(jnp.float32)
    low_o = summed[:, local_width:]
    spread_o = (pick_bf[:, :, None] * low_o[:, None, :]).reshape(tok_count, req_count * rank_dim)
    delta_o = jnp.dot(
        spread_o,
        sel_oup.reshape(req_count * rank_dim, local_width),
        preferred_element_type=jnp.float32,
    )
    own_rows = lax.dynamic_slice_in_dim(tokens, tp_id * local_width, local_width, 1).astype(
        jnp.float32
    )
    layer_out = (own_rows + base_out + delta_o).astype(jnp.bfloat16)
    page_row = page_table[0]
    page_count = page_row.shape[0]
    numbers = jnp.arange(page_count, dtype=jnp.int32)
    inverse = jnp.sum(jnp.where(page_row[:, None] == numbers[None, :], numbers[:, None], 0), axis=0)
    both_blocks = jnp.stack(
        [
            key_rows.reshape(page_count, PAGE, local_width),
            value_rows.reshape(page_count, PAGE, local_width),
        ],
        axis=1,
    )
    kv_pages = jnp.take(both_blocks, inverse, axis=0)
    return (layer_out, kv_pages)


def solution(mesh):
    return jax.shard_map(
        local,
        mesh=mesh,
        in_specs=(
            P("grp", None),
            P(),
            P(None, None, "tp"),
            P("tp", None),
            P("grp", "tp", None),
            P("grp", None, None, "tp"),
            P("grp", "tp", None),
            P("grp", None, "tp"),
            P(),
            P(),
            P(),
            P("grp", None),
        ),
        out_specs=(P("grp", "tp"), P("grp", None, None, "tp")),
        check_vma=False,
    )
```

profile of v0, /device:TPU:4, one launch (start us, length us, event | category | flops | bytes accessed | tf_op | source)
XLA Modules:
  0.0 312.4 jit_solution(5977130857267515130)
XLA Ops:
  9.5 1.3 gather_fusion.1
  14.0 1.2 gather_fusion.2
  19.6 3.1 fusion.2
  23.4 4.7 %copy.62 = bf16[2048,3,256]{0,2,1:T(8,128)(2,1)} copy(bf16[2048,3,256]{2,0,1:T(8,128)(2,1)} %param.14) | data formatting | bytes 6291456 | tf_op args[2]
  28.6 3.5 %fusion.4 = bf16[1024,2048]{1,0:T(8,128)(2,1)S(1)} fusion(bf16[1024,2048]{1,0:T(8,128)(2,1)} %param.12, f32[2048]{0:T(1024)S(1)} %copy-done.7, f32[1024]{0:T(1024)S(1)} %add_rsqrt_fusion), kind=kLoop, calls=%fused_computation.14 | loop fusion | flops 8388608 | bytes 8400896 | tf_op jit(solution)/shard_map/convert_element_type | solution.py:60
  32.2 1.9 copy-done.2
  34.1 5.1 %fusion.9 = f32[1024,3,256]{0,2,1:T(8,128)} fusion(bf16[1024,2048]{1,0:T(8,128)(2,1)S(1)} %fusion.4, bf16[2048,3,256]{0,2,1:T(8,128)(2,1)S(1)} %copy-done.3), kind=kOutput, calls=%fused_computation.21 | convolution fusion | flops 3221225472 | bytes 10485760 | tf_op jit(solution)/shard_map/dot_general | solution.py:131
  39.2 129.0 %all-reduce.2.cloned.1.call-done = bf16[16,32768]{1,0:T(8,128)(2,1)} async-done(((bf16[16,32768]{1,0:T(8,128)(2,1)}), bf16[16,32768]{1,0:T(8,128)(2,1)}) %all-reduce.2.cloned.1.call-update) | async-done | bytes 1048592 | tf_op jit(solution)/shard_map/psum | solution.py:46
  168.2 2.4 gather_fusion.3
  172.6 1.4 fusion.21
  174.2 1.5 pad_add_fusion
  175.7 1.6 collective-permute-start.1
  177.3 3.0 multiply_cosine_fusion
  180.3 2.8 collective-permute-done.1
  183.1 3.3 %collective-permute-start.2 = (f32[1024,48]{0,1:T(8,128)S(1)}, f32[1024,48]{0,1:T(8,128)S(1)}, u32[]{:S(2)}, u32[]{:S(2)}) collective-permute-start(f32[1024,48]{0,1:T(8,128)S(1)} %add.163), channel_id=1, source_target_pairs={{0,4},{1,5},{2,6},{3,7},{4,0},{5,1},{6,2},{7,3},{8,12},{9,13},{10,... | collective-permute-start | bytes 589832 | tf_op jit(solution)/shard_map/ppermute | solution.py:27
  187.6 3.7 %collective-permute-done.2 = f32[1024,48]{0,1:T(8,128)S(1)} collective-permute-done((f32[1024,48]{0,1:T(8,128)S(1)}, f32[1024,48]{0,1:T(8,128)S(1)}, u32[]{:S(2)}, u32[]{:S(2)}) %collective-permute-start.2) | collective-permute-done | bytes 196640 | tf_op jit(solution)/shard_map/ppermute | solution.py:27
  191.3 2.5 bitcast_add_fusion
  197.1 3.2 %collective-permute-start.3 = (bf16[1024,256]{0,1:T(8,128)(2,1)}, bf16[1024,256]{0,1:T(8,128)(2,1)}, u32[]{:S(2)}, u32[]{:S(2)}) collective-permute-start(bf16[1024,256]{0,1:T(8,128)(2,1)} %bitcast.106), channel_id=1, source_target_pairs={{0,8},{8,16},{16,24},{24,32},{32,40},{40,48},{48,56},{56,64},{64,7... | collective-permute-start | bytes 1572872 | tf_op jit(solution)/shard_map/ppermute | solution.py:16
  200.3 1.6 copy.89
  201.9 1.6 multiply_subtract_fusion
  204.8 4.1 %collective-permute-start.4 = (bf16[1024,256]{0,1:T(8,128)(2,1)}, bf16[1024,256]{0,1:T(8,128)(2,1)}, u32[]{:S(2)}, u32[]{:S(2)}) collective-permute-start(bf16[1024,256]{0,1:T(8,128)(2,1)} %bitcast.29), channel_id=1, source_target_pairs={{0,8},{8,16},{16,24},{24,32},{32,40},{40,48},{48,56},{56,64},{64,7... | collective-permute-start | bytes 1572872 | tf_op jit(solution)/shard_map/ppermute | solution.py:16
  209.0 1.3 slice_bitcast_fusion
  210.3 2.6 subtract_convert_fusion
  212.9 10.3 %collective-permute-done.4 = bf16[1024,256]{0,1:T(8,128)(2,1)} collective-permute-done((bf16[1024,256]{0,1:T(8,128)(2,1)}, bf16[1024,256]{0,1:T(8,128)(2,1)}, u32[]{:S(2)}, u32[]{:S(2)}) %collective-permute-start.4) | collective-permute-done | bytes 524320 | tf_op jit(solution)/shard_map/ppermute | solution.py:16
  223.2 1.3 copy.72
  224.5 10.8 %fusion.49 = (f32[2,1024]{1,0:T(2,128)S(1)}, f32[2,1024,2048]{2,1,0:T(8,128)}) fusion(pred[1024,2048]{1,0:T(8,128)(4,1)} %pad_add_fusion, bf16[1024,2,128]{2,0,1:T(8,128)(2,1)S(1)} %maximum_convert_fusion, bf16[1024,2,128]{2,0,1:T(8,128)(2,1)S(1)} %copy.72, bf16[1024,2,64]{2,0,1:T(8,128)(2,1)} %get-tuple-element.7, bf16[1024,2,64]{2,0,1:T(8,128)(2,1)} %get-tuple-element.6), kind=kOutput, calls=%fused_computation.127 | convolution fusion | flops 1093666816 | bytes 20455424 | tf_op jit(solution)/shard_map/sub | solution.py:159
  235.3 8.9 %fusion.16 = bf16[2,128,1024]{2,1,0:T(8,128)(2,1)S(1)} fusion(f32[2,1024,2048]{2,1,0:T(8,128)} %get-tuple-element.23, f32[2,1024]{1,0:T(2,128)S(1)} %get-tuple-element.22, bf16[1024,2,128]{0,2,1:T(8,128)(2,1)S(1)} %slice_bitcast_fusion, bf16[1024,2,128]{0,2,1:T(8,128)(2,1)} %bitcast.22), kind=kOutput, calls=%fused_computation.32 | convolution fusion | flops 1084489728 | bytes 18358272 | tf_op jit(solution)/shard_map/hts,shd->thd/dot_general | solution.py:161
  244.5 3.2 %convolution_convert_fusion = bf16[1024,2048]{1,0:T(8,128)(2,1)} fusion(bf16[1024,256]{0,1:T(8,128)(2,1)S(1)} %bitcast.104, bf16[256,2048]{1,0:T(8,128)(2,1)S(1)} %copy-done), kind=kOutput, calls=%fused_computation.25 | convolution fusion | flops 1075838976 | bytes 5767168 | tf_op jit(solution)/shard_map/dot_general | solution.py:165
  247.7 6.4 %copy.82 = bf16[1024,2048]{0,1:T(8,128)(2,1)} copy(bf16[1024,2048]{1,0:T(8,128)(2,1)} %convolution_convert_fusion) | data formatting | bytes 8388608 | tf_op jit(solution)/shard_map/reshape | solution.py:171
  254.1 4.7 %pad_maximum_fusion = bf16[1024,8,272]{0,2,1:T(8,128)(2,1)} fusion(bf16[1024,8,16]{0,2,1:T(8,128)(2,1)S(1)} %broadcast_in_dim.158, bf16[1024,8,256]{0,2,1:T(8,128)(2,1)} %bitcast.97), kind=kLoop, calls=%fused_computation.20 | loop fusion | flops 8912896 | bytes 8912896 | tf_op jit(solution)/shard_map/concatenate | solution.py:169
  264.7 36.7 %reduce-scatter.4.cloned.1.call-done = bf16[272,1024]{1,0:T(8,128)(2,1)} async-done(((bf16[2176,1024]{1,0:T(8,128)(2,1)}), bf16[272,1024]{1,0:T(8,128)(2,1)}) %reduce-scatter.4.cloned.1.call-update) | async-done | bytes 557072
  303.4 2.2 fusion.15
  (106 shorter events, 25.6 us)
Async XLA Ops:
  7.2 237.3 %copy-start = (bf16[256,2048]{1,0:T(8,128)(2,1)S(1)}, bf16[256,2048]{1,0:T(8,128)(2,1)}, u32[]{:S(2)}) copy-start(bf16[256,2048]{1,0:T(8,128)(2,1)} %param.15) | copy-start | bytes 3145732
  7.2 161.0 %all-reduce.2.cloned.1.call-start = ((), (), s32[]{:S(2)}) async-start(), calls=%async_computation.1 | async-start | bytes 2097152 | tf_op jit(solution)/shard_map/psum | solution.py:46
  14.0 2.5 copy-start.8
  14.0 2.5 copy-start.9
  16.4 284.9 %reduce-scatter.4.cloned.1.call-start = ((), (), s32[]{:S(2)}) async-start(), calls=%async_computation.2 | async-start | bytes 5013504
  22.7 5.9 %copy-start.7 = (f32[2048]{0:T(1024)S(1)}, f32[2048]{0:T(1024)}, u32[]{:S(2)}) copy-start(f32[2048]{0:T(1024)} %param.13) | copy-start | bytes 24580
  28.6 5.4 %copy-start.3 = (bf16[2048,3,256]{0,2,1:T(8,128)(2,1)S(1)}, bf16[2048,3,256]{0,2,1:T(8,128)(2,1)}, u32[]{:S(2)}) copy-start(bf16[2048,3,256]{0,2,1:T(8,128)(2,1)} %copy.62) | copy-start | bytes 9437188
  32.1 1.9 copy-start.2
  170.8 0.7 copy-start.5
  172.6 14.6 %copy-start.6 = (bf16[4,12288]{1,0:T(4,128)(2,1)S(1)}, bf16[4,12288]{1,0:T(4,128)(2,1)}, u32[]{:S(2)}) copy-start(bf16[4,12288]{1,0:T(4,128)(2,1)} %get-tuple-element.13) | copy-start | bytes 294916
  174.1 1.6 collective-permute-start
  175.7 7.4 %collective-permute-start.1 = (f32[1024,48]{0,1:T(8,128)S(1)}, f32[1024,48]{0,1:T(8,128)S(1)}, u32[]{:S(2)}, u32[]{:S(2)}) collective-permute-start(f32[1024,48]{0,1:T(8,128)S(1)} %add.162), channel_id=1, source_target_pairs={{0,2},{1,3},{2,0},{3,1},{4,6},{5,7},{6,4},{7,5},{8,10},{9,11},{10,... | collective-permute-start | bytes 589832 | tf_op jit(solution)/shard_map/ppermute | solution.py:27
  183.1 8.2 %collective-permute-start.2 = (f32[1024,48]{0,1:T(8,128)S(1)}, f32[1024,48]{0,1:T(8,128)S(1)}, u32[]{:S(2)}, u32[]{:S(2)}) collective-permute-start(f32[1024,48]{0,1:T(8,128)S(1)} %add.163), channel_id=1, source_target_pairs={{0,4},{1,5},{2,6},{3,7},{4,0},{5,1},{6,2},{7,3},{8,12},{9,13},{10,... | collective-permute-start | bytes 589832 | tf_op jit(solution)/shard_map/ppermute | solution.py:27
  193.8 1.8 copy-start.1
  197.1 38.1 %collective-permute-start.3 = (bf16[1024,256]{0,1:T(8,128)(2,1)}, bf16[1024,256]{0,1:T(8,128)(2,1)}, u32[]{:S(2)}, u32[]{:S(2)}) collective-permute-start(bf16[1024,256]{0,1:T(8,128)(2,1)} %bitcast.106), channel_id=1, source_target_pairs={{0,8},{8,16},{16,24},{24,32},{32,40},{40,48},{48,56},{56,64},{64,7... | collective-permute-start | bytes 1572872 | tf_op jit(solution)/shard_map/ppermute | solution.py:16
  204.8 18.3 %collective-permute-start.4 = (bf16[1024,256]{0,1:T(8,128)(2,1)}, bf16[1024,256]{0,1:T(8,128)(2,1)}, u32[]{:S(2)}, u32[]{:S(2)}) collective-permute-start(bf16[1024,256]{0,1:T(8,128)(2,1)} %bitcast.29), channel_id=1, source_target_pairs={{0,8},{8,16},{16,24},{24,32},{32,40},{40,48},{48,56},{56,64},{64,7... | collective-permute-start | bytes 1572872 | tf_op jit(solution)/shard_map/ppermute | solution.py:16
  258.8 0.7 copy-start.10
  258.8 1.3 copy-start.4
Sparse Core Ops, SparseCore 0:
  16.6 151.6 all-reduce.1
  259.0 42.3 reduce-scatter.3
where the time goes:
time: 314 us; the launch traced here: 312 us
  waiting for transfers between devices  183 us (58%)
  local copies, waits for them, and re-layouts  40.9 us (13%)
  matrix products  34.3 us (11%)
  other arithmetic  26.4 us (8%)
  between operations  15.9 us (5%)
  starting transfers between devices  12.3 us (4%)
    psum x1, waiting for transfers between devices, fetch_adapters(): compact = lax.psum(compact, 'grp')  129 us
    unnamed x3, waiting for transfers between devices  36.7 us
    unnamed x34, local copies, waits for them, and re-layouts  15.3 us
    sub x1, matrix products, local(): weights = jnp.exp(scores - row_top)  10.8 us
    ppermute x2, waiting for transfers between devices, shifted(): return lax.ppermute(block, axis, route)  10.3 us
    dot_general x1, matrix products, local(): jnp.einsum('hts,shd->thd', weights_bf, value_all, preferred_element_type=...  8.93 us
    ppermute x2, starting transfers between devices, shifted(): return lax.ppermute(block, axis, route)  7.3 us
    ppermute x3, waiting for transfers between devices, xor_allreduce(): value = value + lax.ppermute(value, axis, route)  6.53 us
  transfers between devices with their start and end apart: 7, of which 5 were waited for; matrix products, arithmetic and copies ran while one was open for 16% of the time, Pallas kernels for 0%

commit v1 on v0

--- a/solution.py
+++ b/solution.py
@@ -8,6 +8,17 @@
 PAGE = 128
 EPSILON = 1e-05
 THETA = 10000.0
+
+
+def push_sectors(obj, link_axis):
+    amount_of = jax.lax.axis_size(link_axis)
+    res = lambda o_now: [(jj, jj ^ o_now) for jj in range(amount_of)]
+    wide_out = obj
+    for p in range(amount_of.bit_length() - 1):
+        tile_out = res(1 << p)
+        heard = jax.lax.ppermute(wide_out, link_axis, tile_out)
+        wide_out = wide_out + heard
+    return wide_out
 
 
 def shifted(block, axis, distance):
@@ -43,7 +54,7 @@
     local_idx = slots % held
     flat = jnp.concatenate([s.reshape(held, -1) for s in stores], axis=1)
     compact = jnp.where(mine[:, None], jnp.take(flat, local_idx, axis=0), jnp.zeros((), flat.dtype))
-    compact = lax.psum(compact, "grp")
+    compact = push_sectors(compact, "grp")
     mine_rows = jnp.take(compact, rank[wanted], axis=0)
     out = []
     at = 0

time: 314 us -> 334 us (1.064)
  starting transfers between devices: 12.3 us -> 23.8 us
  waiting for transfers between devices: 183 us -> 192 us
  other arithmetic: 26.4 us -> 29.9 us
  local copies, waits for them, and re-layouts: 40.9 us -> 37.5 us
    ppermute x0 -> x5, waiting for transfers between devices: none -> 138 us  [push_sectors(): heard = jax.lax.ppermute(wide_out, link_axis, tile_out)]
    psum x1 -> x0, waiting for transfers between devices: 129 us -> none  [fetch_adapters(): compact = lax.psum(compact, 'grp')]
    ppermute x0 -> x5, starting transfers between devices: none -> 13.5 us  [push_sectors(): heard = jax.lax.ppermute(wide_out, link_axis, tile_out)]
    add x0 -> x5, other arithmetic: none -> 3.61 us  [push_sectors(): wide_out = wide_out + heard]
    unnamed x34 -> x36, local copies, waits for them, and re-layouts: 15.3 us -> 13.4 us
    unnamed x3 -> x2, waiting for transfers between devices: 36.7 us -> 34.9 us
  transfers between devices with their start and end apart: 7 -> 11, of which waited for: 5 -> 9; matrix products, arithmetic and copies ran while one was open for 16% -> 15% of each run, Pallas kernels for 0% -> 0%
where the time goes in v1:
time: 334 us; the launch traced here: 333 us
  waiting for transfers between devices  192 us (57%)
  local copies, waits for them, and re-layouts  37.5 us (11%)
  matrix products  34.4 us (10%)
  other arithmetic  29.9 us (9%)
  starting transfers between devices  23.8 us (7%)
  between operations  15.9 us (5%)
    ppermute x5, waiting for transfers between devices, push_sectors(): heard = jax.lax.ppermute(wide_out, link_axis, tile_out)  138 us
    unnamed x2, waiting for transfers between devices  34.9 us
    ppermute x5, starting transfers between devices, push_sectors(): heard = jax.lax.ppermute(wide_out, link_axis, tile_out)  13.5 us
    unnamed x36, local copies, waits for them, and re-layouts  13.4 us
    ppermute x2, waiting for transfers between devices, shifted(): return lax.ppermute(block, axis, route)  12.3 us
    sub x1, matrix products, local(): weights = jnp.exp(scores - row_top)  10.8 us
    dot_general x1, matrix products, local(): jnp.einsum('hts,shd->thd', weights_bf, value_all, preferred_element_type=...  8.93 us
  transfers between devices with their start and end apart: 11, of which 9 were waited for; matrix products, arithmetic and copies ran while one was open for 15% of the time, Pallas kernels for 0%

profile of v1, /device:TPU:4, one launch (start us, length us, event | category | flops | bytes accessed | tf_op | source)
XLA Modules:
  0.0 332.9 jit_solution(16684028391361807839)
XLA Ops:
  18.5 22.1 %collective-permute-done = bf16[16,32768]{1,0:T(8,128)(2,1)} collective-permute-done((bf16[16,32768]{1,0:T(8,128)(2,1)S(1)}, bf16[16,32768]{1,0:T(8,128)(2,1)}, u32[]{:S(2)}, u32[]{:S(2)}) %collective-permute-start) | collective-permute-done | bytes 1048608 | tf_op jit(solution)/shard_map/ppermute | solution.py:19
  43.7 23.9 %collective-permute-done.1 = bf16[16,32768]{1,0:T(8,128)(2,1)S(1)} collective-permute-done((bf16[16,32768]{1,0:T(8,128)(2,1)S(1)}, bf16[16,32768]{1,0:T(8,128)(2,1)S(1)}, u32[]{:S(2)}, u32[]{:S(2)}) %collective-permute-start.1) | collective-permute-done | bytes 1048608 | tf_op jit(solution)/shard_map/ppermute | solution.py:19
  67.8 2.0 collective-permute-start.2
  69.9 3.1 fusion.2
  73.5 17.8 %collective-permute-done.2 = bf16[16,32768]{1,0:T(8,128)(2,1)S(1)} collective-permute-done((bf16[16,32768]{1,0:T(8,128)(2,1)S(1)}, bf16[16,32768]{1,0:T(8,128)(2,1)S(1)}, u32[]{:S(2)}, u32[]{:S(2)}) %collective-permute-start.2) | collective-permute-done | bytes 1048608 | tf_op jit(solution)/shard_map/ppermute | solution.py:19
  91.6 3.4 %collective-permute-start.3 = (bf16[16,32768]{1,0:T(8,128)(2,1)S(1)}, bf16[16,32768]{1,0:T(8,128)(2,1)}, u32[]{:S(2)}, u32[]{:S(2)}) collective-permute-start(bf16[16,32768]{1,0:T(8,128)(2,1)S(1)} %add.176), channel_id=1, source_target_pairs={{0,64},{8,72},{16,80},{24,88},{32,96},{40,104},{48,112},{56,120},{... | collective-permute-start | bytes 3145736 | tf_op jit(solution)/shard_map/ppermute | solution.py:19
  94.9 4.7 %copy.62 = bf16[2048,3,256]{0,2,1:T(8,128)(2,1)} copy(bf16[2048,3,256]{2,0,1:T(8,128)(2,1)} %param.14) | data formatting | bytes 6291456 | tf_op args[2]
  99.6 1.6 fusion.11
  101.2 3.4 %fusion.4 = bf16[1024,2048]{1,0:T(8,128)(2,1)S(1)} fusion(bf16[1024,2048]{1,0:T(8,128)(2,1)} %param.12, f32[2048]{0:T(1024)S(1)} %copy-done.8, f32[1024]{0:T(1024)S(1)} %add_rsqrt_fusion), kind=kLoop, calls=%fused_computation.14 | loop fusion | flops 8388608 | bytes 8400896 | tf_op jit(solution)/shard_map/convert_element_type | solution.py:71
  104.5 33.7 %collective-permute-done.3 = bf16[16,32768]{1,0:T(8,128)(2,1)} collective-permute-done((bf16[16,32768]{1,0:T(8,128)(2,1)S(1)}, bf16[16,32768]{1,0:T(8,128)(2,1)}, u32[]{:S(2)}, u32[]{:S(2)}) %collective-permute-start.3) | collective-permute-done | bytes 1048608 | tf_op jit(solution)/shard_map/ppermute | solution.py:19
  139.7 6.5 %collective-permute-start.4 = (bf16[16,32768]{1,0:T(8,128)(2,1)S(1)}, bf16[16,32768]{1,0:T(8,128)(2,1)S(1)}, u32[]{:S(2)}, u32[]{:S(2)}) collective-permute-start(bf16[16,32768]{1,0:T(8,128)(2,1)S(1)} %add.177), channel_id=1, source_target_pairs={{0,128},{8,136},{16,144},{24,152},{32,160},{40,168},{48,176},{56,1... | collective-permute-start | bytes 3145736 | tf_op jit(solution)/shard_map/ppermute | solution.py:19
  146.2 5.1 %fusion.9 = f32[1024,3,256]{0,2,1:T(8,128)} fusion(bf16[1024,2048]{1,0:T(8,128)(2,1)S(1)} %fusion.4, bf16[2048,3,256]{0,2,1:T(8,128)(2,1)S(1)} %copy-done.4), kind=kOutput, calls=%fused_computation.21 | convolution fusion | flops 3221225472 | bytes 10485760 | tf_op jit(solution)/shard_map/dot_general | solution.py:142
  151.3 40.6 %collective-permute-done.4 = bf16[16,32768]{1,0:T(8,128)(2,1)S(1)} collective-permute-done((bf16[16,32768]{1,0:T(8,128)(2,1)S(1)}, bf16[16,32768]{1,0:T(8,128)(2,1)S(1)}, u32[]{:S(2)}, u32[]{:S(2)}) %collective-permute-start.4) | collective-permute-done | bytes 1048608 | tf_op jit(solution)/shard_map/ppermute | solution.py:19
  198.1 1.7 collective-permute-start.6
  199.8 3.0 multiply_cosine_fusion
  202.8 2.7 collective-permute-done.6
  205.5 3.3 collective-permute-start.7
  210.0 3.5 %collective-permute-done.7 = f32[1024,48]{0,1:T(8,128)S(1)} collective-permute-done((f32[1024,48]{0,1:T(8,128)S(1)}, f32[1024,48]{0,1:T(8,128)S(1)}, u32[]{:S(2)}, u32[]{:S(2)}) %collective-permute-start.7) | collective-permute-done | bytes 196640 | tf_op jit(solution)/shard_map/ppermute | solution.py:38
  213.5 2.5 bitcast_add_fusion
  219.4 3.1 collective-permute-start.8
  222.5 1.6 copy.89
  224.0 1.6 multiply_subtract_fusion
  227.0 2.1 collective-permute-start.9
  230.4 2.6 subtract_convert_fusion
  233.1 12.3 %collective-permute-done.9 = bf16[1024,256]{0,1:T(8,128)(2,1)} collective-permute-done((bf16[1024,256]{0,1:T(8,128)(2,1)}, bf16[1024,256]{0,1:T(8,128)(2,1)}, u32[]{:S(2)}, u32[]{:S(2)}) %collective-permute-start.9) | collective-permute-done | bytes 524320 | tf_op jit(solution)/shard_map/ppermute | solution.py:27
  246.7 10.8 %fusion.49 = (f32[2,1024]{1,0:T(2,128)S(1)}, f32[2,1024,2048]{2,1,0:T(8,128)}) fusion(pred[1024,2048]{1,0:T(8,128)(4,1)} %pad_add_fusion, bf16[1024,2,128]{2,0,1:T(8,128)(2,1)S(1)} %maximum_convert_fusion, bf16[1024,2,128]{2,0,1:T(8,128)(2,1)S(1)} %copy.72, bf16[1024,2,64]{2,0,1:T(8,128)(2,1)} %get-tuple-element.7, bf16[1024,2,64]{2,0,1:T(8,128)(2,1)} %get-tuple-element.6), kind=kOutput, calls=%fused_computation.127 | convolution fusion | flops 1093666816 | bytes 20455424 | tf_op jit(solution)/shard_map/sub | solution.py:170
  257.5 8.9 %fusion.16 = bf16[2,128,1024]{2,1,0:T(8,128)(2,1)S(1)} fusion(f32[2,1024,2048]{2,1,0:T(8,128)} %get-tuple-element.23, f32[2,1024]{1,0:T(2,128)S(1)} %get-tuple-element.22, bf16[1024,2,128]{0,2,1:T(8,128)(2,1)S(1)} %slice_bitcast_fusion, bf16[1024,2,128]{0,2,1:T(8,128)(2,1)} %bitcast.22), kind=kOutput, calls=%fused_computation.32 | convolution fusion | flops 1084489728 | bytes 18358272 | tf_op jit(solution)/shard_map/hts,shd->thd/dot_general | solution.py:172
  266.7 3.2 convolution_convert_fusion
  269.9 6.4 %copy.82 = bf16[1024,2048]{0,1:T(8,128)(2,1)} copy(bf16[1024,2048]{1,0:T(8,128)(2,1)} %convolution_convert_fusion) | data formatting | bytes 8388608 | tf_op jit(solution)/shard_map/reshape | solution.py:182
  276.4 4.7 %pad_maximum_fusion = bf16[1024,8,272]{0,2,1:T(8,128)(2,1)} fusion(bf16[1024,8,16]{0,2,1:T(8,128)(2,1)S(1)} %broadcast_in_dim.158, bf16[1024,8,256]{0,2,1:T(8,128)(2,1)} %bitcast.97), kind=kLoop, calls=%fused_computation.20 | loop fusion | flops 8912896 | bytes 8912896 | tf_op jit(solution)/shard_map/concatenate | solution.py:180
  286.9 34.9 %reduce-scatter.4.cloned.1.call-done = bf16[272,1024]{1,0:T(8,128)(2,1)} async-done(((bf16[2176,1024]{1,0:T(8,128)(2,1)}), bf16[272,1024]{1,0:T(8,128)(2,1)}) %reduce-scatter.4.cloned.1.call-update) | async-done | bytes 557072
  323.9 2.2 fusion.15
  (120 shorter events, 38.1 us)
Async XLA Ops:
  7.2 259.5 %copy-start = (bf16[256,2048]{1,0:T(8,128)(2,1)S(1)}, bf16[256,2048]{1,0:T(8,128)(2,1)}, u32[]{:S(2)}) copy-start(bf16[256,2048]{1,0:T(8,128)(2,1)} %param.15) | copy-start | bytes 3145732
  7.2 314.6 %reduce-scatter.4.cloned.1.call-start = ((), (), s32[]{:S(2)}) async-start(), calls=%async_computation.1 | async-start | bytes 5013504
  14.0 2.7 copy-start.9
  14.0 2.7 copy-start.10
  15.4 25.1 %collective-permute-start = (bf16[16,32768]{1,0:T(8,128)(2,1)S(1)}, bf16[16,32768]{1,0:T(8,128)(2,1)}, u32[]{:S(2)}, u32[]{:S(2)}) collective-permute-start(bf16[16,32768]{1,0:T(8,128)(2,1)S(1)} %select_select_fusion), channel_id=1, source_target_pairs={{0,8},{8,0},{16,24},{24,16},{32,40},{40,32},{48,56},{56,48},{64,72... | collective-permute-start | bytes 3145736 | tf_op jit(solution)/shard_map/ppermute | solution.py:19
  42.0 25.6 %collective-permute-start.1 = (bf16[16,32768]{1,0:T(8,128)(2,1)S(1)}, bf16[16,32768]{1,0:T(8,128)(2,1)S(1)}, u32[]{:S(2)}, u32[]{:S(2)}) collective-permute-start(bf16[16,32768]{1,0:T(8,128)(2,1)S(1)} %fusion.59), channel_id=1, source_target_pairs={{0,16},{8,24},{16,0},{24,8},{32,48},{40,56},{48,32},{56,40},{64,80... | collective-permute-start | bytes 3145736 | tf_op jit(solution)/shard_map/ppermute | solution.py:19
  67.8 23.5 %collective-permute-start.2 = (bf16[16,32768]{1,0:T(8,128)(2,1)S(1)}, bf16[16,32768]{1,0:T(8,128)(2,1)S(1)}, u32[]{:S(2)}, u32[]{:S(2)}) collective-permute-start(bf16[16,32768]{1,0:T(8,128)(2,1)S(1)} %add.175), channel_id=1, source_target_pairs={{0,32},{8,40},{16,48},{24,56},{32,0},{40,8},{48,16},{56,24},{64,96... | collective-permute-start | bytes 3145736 | tf_op jit(solution)/shard_map/ppermute | solution.py:19
  91.5 9.6 %copy-start.8 = (f32[2048]{0:T(1024)S(1)}, f32[2048]{0:T(1024)}, u32[]{:S(2)}) copy-start(f32[2048]{0:T(1024)} %param.13) | copy-start | bytes 24580
  91.6 46.7 %collective-permute-start.3 = (bf16[16,32768]{1,0:T(8,128)(2,1)S(1)}, bf16[16,32768]{1,0:T(8,128)(2,1)}, u32[]{:S(2)}, u32[]{:S(2)}) collective-permute-start(bf16[16,32768]{1,0:T(8,128)(2,1)S(1)} %add.176), channel_id=1, source_target_pairs={{0,64},{8,72},{16,80},{24,88},{32,96},{40,104},{48,112},{56,120},{... | collective-permute-start | bytes 3145736 | tf_op jit(solution)/shard_map/ppermute | solution.py:19
  101.2 45.0 %copy-start.4 = (bf16[2048,3,256]{0,2,1:T(8,128)(2,1)S(1)}, bf16[2048,3,256]{0,2,1:T(8,128)(2,1)}, u32[]{:S(2)}) copy-start(bf16[2048,3,256]{0,2,1:T(8,128)(2,1)} %copy.62) | copy-start | bytes 9437188
  104.5 46.8 %copy-start.2 = (bf16[1024,2048]{1,0:T(8,128)(2,1)}, bf16[1024,2048]{1,0:T(8,128)(2,1)S(1)}, u32[]{:S(2)}) copy-start(bf16[1024,2048]{1,0:T(8,128)(2,1)S(1)} %fusion.4) | copy-start | bytes 12582916
  139.7 52.2 %collective-permute-start.4 = (bf16[16,32768]{1,0:T(8,128)(2,1)S(1)}, bf16[16,32768]{1,0:T(8,128)(2,1)S(1)}, u32[]{:S(2)}, u32[]{:S(2)}) collective-permute-start(bf16[16,32768]{1,0:T(8,128)(2,1)S(1)} %add.177), channel_id=1, source_target_pairs={{0,128},{8,136},{16,144},{24,152},{32,160},{40,168},{48,176},{56,1... | collective-permute-start | bytes 3145736 | tf_op jit(solution)/shard_map/ppermute | solution.py:19
  193.0 3.6 %copy-start.3 = (pred[1024,1024]{1,0:T(8,128)(4,1)S(1)}, pred[1024,1024]{1,0:T(8,128)(4,1)}, u32[]{:S(2)}) copy-start(pred[1024,1024]{1,0:T(8,128)(4,1)} %fusion.11) | copy-start | bytes 3145732
  193.2 0.7 copy-start.6
  194.9 14.6 %copy-start.7 = (bf16[4,12288]{1,0:T(4,128)(2,1)S(1)}, bf16[4,12288]{1,0:T(4,128)(2,1)}, u32[]{:S(2)}) copy-start(bf16[4,12288]{1,0:T(4,128)(2,1)} %get-tuple-element.13) | copy-start | bytes 294916
  196.4 1.7 collective-permute-start.5
  198.1 7.4 %collective-permute-start.6 = (f32[1024,48]{0,1:T(8,128)S(1)}, f32[1024,48]{0,1:T(8,128)S(1)}, u32[]{:S(2)}, u32[]{:S(2)}) collective-permute-start(f32[1024,48]{0,1:T(8,128)S(1)} %add.180), channel_id=1, source_target_pairs={{0,2},{1,3},{2,0},{3,1},{4,6},{5,7},{6,4},{7,5},{8,10},{9,11},{10,... | collective-permute-start | bytes 589832 | tf_op jit(solution)/shard_map/ppermute | solution.py:38
  205.5 8.0 %collective-permute-start.7 = (f32[1024,48]{0,1:T(8,128)S(1)}, f32[1024,48]{0,1:T(8,128)S(1)}, u32[]{:S(2)}, u32[]{:S(2)}) collective-permute-start(f32[1024,48]{0,1:T(8,128)S(1)} %add.181), channel_id=1, source_target_pairs={{0,4},{1,5},{2,6},{3,7},{4,0},{5,1},{6,2},{7,3},{8,12},{9,13},{10,... | collective-permute-start | bytes 589832 | tf_op jit(solution)/shard_map/ppermute | solution.py:38
  216.0 1.8 copy-start.1
  219.4 38.1 %collective-permute-start.8 = (bf16[1024,256]{0,1:T(8,128)(2,1)}, bf16[1024,256]{0,1:T(8,128)(2,1)}, u32[]{:S(2)}, u32[]{:S(2)}) collective-permute-start(bf16[1024,256]{0,1:T(8,128)(2,1)} %bitcast.106), channel_id=1, source_target_pairs={{0,8},{8,16},{16,24},{24,32},{32,40},{40,48},{48,56},{56,64},{64,7... | collective-permute-start | bytes 1572872 | tf_op jit(solution)/shard_map/ppermute | solution.py:27
  227.0 18.4 %collective-permute-start.9 = (bf16[1024,256]{0,1:T(8,128)(2,1)}, bf16[1024,256]{0,1:T(8,128)(2,1)}, u32[]{:S(2)}, u32[]{:S(2)}) collective-permute-start(bf16[1024,256]{0,1:T(8,128)(2,1)} %bitcast.29), channel_id=1, source_target_pairs={{0,8},{8,16},{16,24},{24,32},{32,40},{40,48},{48,56},{56,64},{64,7... | collective-permute-start | bytes 1572872 | tf_op jit(solution)/shard_map/ppermute | solution.py:27
  281.1 0.7 copy-start.11
  281.1 1.3 copy-start.5
Sparse Core Ops, SparseCore 0:
  281.2 40.5 reduce-scatter.3
